TPU v7x, 128 devices: a whole 4x4x4 slice. The times are simulated.
128 devices in a mesh: req: 8 (over y, core), exp: 16 (over z, x).
Axes of the slice: x: 4, y: 4, z: 4, core: 2. Of those that a mesh axis runs over, the one named last changes fastest.
Arguments:
- hidden: bfloat16 [16384, 2560], P(('req', 'exp')), may hold values from -1.5 to 1.5
- queries: bfloat16 [16384, 1280], P(('req', 'exp')), may hold values from -100 to 100
- suffix_kv: bfloat16 [16384, 512], P(('req', 'exp')), may hold values from -24 to 24
- lengths: int32 [8, 4], P('req'), may hold values from 1 to 1024, 2048 in all within a row
- page_table: int32 [8, 4, 32], P('req'), may hold values from 0 to 55
- page_pool: bfloat16 [56, 128, 512], P('req'), may hold values from -24 to 24
- w_out: bfloat16 [1280, 2560], replicated, may hold values from -0.15625 to 0.15625
- w_router: bfloat16 [2560, 64], replicated, may hold values from -5 to 5
- routes: int32 [16384, 6], P(('req', 'exp')), may hold values from 0 to 63, all different within a row; in each aligned block of 128 rows (0 to 127, 128 to 255, ...) at most 15 rows name the same one
- w_gate: bfloat16 [128, 2560, 768], P(('req', 'exp')), may hold values from -0.125 to 0.125
- w_up: bfloat16 [128, 2560, 768], P(('req', 'exp')), may hold values from -0.125 to 0.125
- w_down: bfloat16 [128, 768, 2560], P(('req', 'exp')), may hold values from -0.4375 to 0.4375
Outputs:
- layer_out: bfloat16 [16384, 2560], P(('req', 'exp'))
Inputs may be any that keep to these rules, and one draw needn't show every extreme that they name: `lengths`: each row sums to 2048; its largest entry is exactly 1024. `page_table`: a page may appear in several prefixes and more than once in one. `routes`: the 6 experts of a token are distinct; among the rows of one device no expert is named more than 15 times, a bound that some block reaches.
All inputs are finite; a program needn't handle non-finite values.
Results may differ from a plain program's by a relative error of at most 0.022.
Values may be sent and summed in bfloat16 or wider, within the bound.
No kernel may reach another device: no remote copies, remote signals or barrier semaphores. Data moves between devices by JAX's collectives and lax.ppermute only.
A program may use at most 192 MiB of HBM per device.

v0:
```python
import math
import jax
import jax.numpy as jnp
from jax import lax
from jax.sharding import PartitionSpec as P

D = 2560
QUERY_HEADS = 10
KEY_VALUE_HEADS = 2
HEAD_SIZE = 128
TOP = 6
PAGE_TOKENS = 128
NEGATIVE_MASK = -1e30
EPS = 1e-06


def fold_scores(carry, query_matrix, key_rows, value_rows, weights):
    scores = jnp.einsum(
        "tgrd,kgd->tgrk", query_matrix, key_rows, preferred_element_type=jnp.float32
    ) * (1.0 / math.sqrt(HEAD_SIZE))
    running_maximum, grand_total, summed_output = carry
    live = weights[:, None, None, :] > 0
    fresh = jnp.maximum(running_maximum, jnp.max(jnp.where(live, scores, NEGATIVE_MASK), axis=-1))
    expo = jnp.where(live, jnp.exp(scores - fresh[..., None]), 0.0) * weights[:, None, None, :]
    decay = jnp.exp(running_maximum - fresh)
    grand_total = decay * grand_total + jnp.sum(expo, axis=-1)
    summed_output = decay[..., None] * summed_output + jnp.einsum(
        "tgrk,kgd->tgrd", expo.astype(jnp.bfloat16), value_rows, preferred_element_type=jnp.float32
    )
    return (fresh, grand_total, summed_output)


def empty_carry(token_count, request_groups):
    return (
        jnp.full((token_count, KEY_VALUE_HEADS, request_groups), NEGATIVE_MASK, jnp.float32),
        jnp.zeros((token_count, KEY_VALUE_HEADS, request_groups), jnp.float32),
        jnp.zeros((token_count, KEY_VALUE_HEADS, request_groups, HEAD_SIZE), jnp.float32),
    )


def on_device(
    hidden,
    queries,
    suffix_kv,
    lengths,
    page_table,
    page_pool,
    w_out,
    w_router,
    routes,
    w_gate,
    w_up,
    w_down,
):
    token_index = hidden.shape[0]
    row_width = KEY_VALUE_HEADS * HEAD_SIZE
    request_groups = QUERY_HEADS // KEY_VALUE_HEADS
    request_count = lax.axis_size("req")
    pool_per_shard = page_pool.shape[0]
    pool_all = pool_per_shard * request_count
    query_matrix = queries.reshape(token_index, KEY_VALUE_HEADS, request_groups, HEAD_SIZE)
    positions = lax.axis_index("exp") * token_index + jnp.arange(token_index, dtype=jnp.int32)
    lens = lengths[0]
    ends = jnp.cumsum(lens)
    starts = ends - lens
    req_of = jnp.sum((positions[:, None] >= ends[None, :]).astype(jnp.int32), axis=1)
    pick = req_of[:, None] == jnp.arange(lens.shape[0], dtype=jnp.int32)[None, :]
    first = jnp.sum(jnp.where(pick, starts[None, :], 0), axis=1)
    counts = jnp.sum(
        (page_table[0][:, :, None] == jnp.arange(pool_all, dtype=jnp.int32)[None, None, :]).astype(
            jnp.float32
        ),
        axis=1,
    )
    query_counts = jnp.dot(pick.astype(jnp.float32), counts, precision=lax.Precision.HIGHEST)
    query_total_set, every_count = (
        lax.all_gather(queries, "req", axis=0, tiled=True),
        lax.all_gather(query_counts.astype(jnp.bfloat16), "req", axis=0, tiled=True),
    )
    query_total_count = query_total_set.shape[0]
    local = lax.dynamic_slice_in_dim(
        every_count, lax.axis_index("req") * pool_per_shard, pool_per_shard, 1
    ).astype(jnp.float32)
    weights = jnp.repeat(local, PAGE_TOKENS, axis=1)
    flattened = page_pool.reshape(pool_per_shard * PAGE_TOKENS, 2 * row_width)
    key_rows = flattened[:, :row_width].reshape(
        pool_per_shard * PAGE_TOKENS, KEY_VALUE_HEADS, HEAD_SIZE
    )
    value_rows = flattened[:, row_width:].reshape(
        pool_per_shard * PAGE_TOKENS, KEY_VALUE_HEADS, HEAD_SIZE
    )
    running_maximum, grand_total, summed_output = fold_scores(
        empty_carry(query_total_count, request_groups),
        query_total_set.reshape(query_total_count, KEY_VALUE_HEADS, request_groups, HEAD_SIZE),
        key_rows,
        value_rows,
        weights,
    )
    peaks, totals, sums = (
        lax.all_to_all(
            running_maximum.reshape(request_count, token_index, KEY_VALUE_HEADS, request_groups),
            "req",
            split_axis=0,
            concat_axis=0,
            tiled=True,
        ),
        lax.all_to_all(
            grand_total.reshape(request_count, token_index, KEY_VALUE_HEADS, request_groups),
            "req",
            split_axis=0,
            concat_axis=0,
            tiled=True,
        ),
        lax.all_to_all(
            summed_output.reshape(
                request_count, token_index, KEY_VALUE_HEADS, request_groups, HEAD_SIZE
            ),
            "req",
            split_axis=0,
            concat_axis=0,
            tiled=True,
        ),
    )
    highest = jnp.max(peaks, axis=0)
    factor = jnp.exp(peaks - highest[None])
    carry = (highest, jnp.sum(factor * totals, axis=0), jnp.sum(factor[..., None] * sums, axis=0))
    segment = lax.all_gather(suffix_kv, "exp", axis=0, tiled=True)
    token_count = segment.shape[0]
    keypos = jnp.arange(token_count, dtype=jnp.int32)
    weights = (
        (keypos[None, :] <= positions[:, None]) & (keypos[None, :] >= first[:, None])
    ).astype(jnp.float32)
    key_rows = segment[:, :row_width].reshape(token_count, KEY_VALUE_HEADS, HEAD_SIZE)
    value_rows = segment[:, row_width:].reshape(token_count, KEY_VALUE_HEADS, HEAD_SIZE)
    running_maximum, grand_total, summed_output = fold_scores(
        carry, query_matrix, key_rows, value_rows, weights
    )
    attended = (
        (summed_output / grand_total[..., None])
        .reshape(token_index, QUERY_HEADS * HEAD_SIZE)
        .astype(jnp.bfloat16)
    )
    projected = jnp.dot(attended, w_out, preferred_element_type=jnp.float32)
    resid = lax.optimization_barrier((hidden.astype(jnp.float32) + projected).astype(jnp.bfloat16))
    resid_f = resid.astype(jnp.float32)
    normed = (resid_f * lax.rsqrt(jnp.mean(resid_f * resid_f, axis=1, keepdims=True) + EPS)).astype(
        jnp.bfloat16
    )
    n_experts = w_router.shape[1]
    logits = jnp.dot(normed, w_router, preferred_element_type=jnp.float32)
    expert_ids = jnp.arange(n_experts, dtype=jnp.int32)
    chosen = jnp.sum(
        jnp.where(routes[:, :, None] == expert_ids[None, None, :], logits[:, None, :], 0.0), axis=2
    )
    gates = jax.nn.softmax(chosen, axis=1)
    capacity = 16
    member = routes[:, :, None] == expert_ids[None, None, :]
    picks = jnp.any(member, axis=1).astype(jnp.float32)
    gate_of = jnp.sum(jnp.where(member, gates[:, :, None], 0.0), axis=1)
    earlier = (
        jnp.arange(token_index, dtype=jnp.int32)[:, None]
        > jnp.arange(token_index, dtype=jnp.int32)[None, :]
    ).astype(jnp.float32)
    rank = jnp.dot(earlier, picks, precision=lax.Precision.HIGHEST).astype(jnp.int32)
    place = jnp.arange(capacity, dtype=jnp.int32)
    select = (picks[None, :, :] > 0) & (rank[None, :, :] == place[:, None, None])
    select = jnp.transpose(select, (2, 0, 1))
    select2 = jnp.broadcast_to(select[:, None], (n_experts, 2, capacity, token_index)).reshape(
        2 * n_experts * capacity, token_index
    )
    outgoing = jnp.dot(
        select2.astype(jnp.bfloat16), normed, preferred_element_type=jnp.float32
    ).astype(jnp.bfloat16)
    outgoing = outgoing.reshape(2 * n_experts, capacity, D)
    rows = lax.all_to_all(outgoing, ("req", "exp"), split_axis=0, concat_axis=0, tiled=True)
    array_shape = rows.shape
    flat_rows = rows.reshape(-1, D)
    gate_part = jnp.dot(flat_rows, w_gate[0], preferred_element_type=jnp.float32)
    up_part = jnp.dot(flat_rows, w_up[0], preferred_element_type=jnp.float32)
    inner = (jax.nn.silu(gate_part) * up_part).astype(jnp.bfloat16)
    returned = lax.all_to_all(
        jnp.dot(inner, w_down[0], preferred_element_type=jnp.float32)
        .astype(jnp.bfloat16)
        .reshape(array_shape),
        ("req", "exp"),
        split_axis=0,
        concat_axis=0,
        tiled=True,
    ).reshape(2 * n_experts * capacity, D)
    weight = jnp.where(
        jnp.transpose(select, (2, 0, 1))[:, :, None, :], gate_of[:, :, None, None], 0.0
    )
    weight = jnp.broadcast_to(weight, (token_index, n_experts, 2, capacity)).reshape(
        token_index, 2 * n_experts * capacity
    )
    high = weight.astype(jnp.bfloat16)
    low = (weight - high.astype(jnp.float32)).astype(jnp.bfloat16)
    moe = jnp.dot(high, returned, preferred_element_type=jnp.float32) + jnp.dot(
        low, returned, preferred_element_type=jnp.float32
    )
    return (resid_f + moe).astype(jnp.bfloat16)


def solution(mesh):
    placed = (
        P(("req", "exp"), None),
        P(("req", "exp"), None),
        P(("req", "exp"), None),
        P("req", None),
        P("req", None, None),
        P("req", None, None),
        P(),
        P(),
        P(("req", "exp"), None),
        P(("req", "exp"), None, None),
        P(("req", "exp"), None, None),
        P(("req", "exp"), None, None),
    )
    return jax.shard_map(
        on_device, mesh=mesh, in_specs=placed, out_specs=P(("req", "exp"), None), check_vma=False
    )
```

profile of v0, /device:TPU:34, one launch (start us, length us, event | category | flops | bytes accessed | tf_op | source)
XLA Modules:
  0.0 531.8 jit_solution(14392213772407807917)
XLA Ops:
  7.4 1.9 copy.140
  9.3 0.8 reduce-window.4
  10.2 0.8 convert_reduce_fusion
  11.0 0.2 convolution_convert_fusion.3
  11.2 12.1 %all_gather.9 = bf16[1024,56]{0,1:T(8,128)(2,1)S(1)} all-gather(bf16[128,56]{0,1:T(8,128)(2,1)S(1)} %convolution_convert_fusion.3), channel_id=1, replica_groups=mesh['req'=8,'exp'=16] {'req'}, dimensions={0}, use_global_device_ids=true | all-gather | bytes 129024 | tf_op jit(solution)/shard_map/all_gather | solution.py:78
  23.4 0.2 bitcast_compare_fusion
  23.6 1.2 fusion.69
  24.8 0.2 copy.139
  25.1 16.3 %all-gather.3.cloned.1.call-done = bf16[1024,1280]{0,1:T(8,128)(2,1)} async-done(((bf16[128,1280]{0,1:T(8,128)(2,1)}), bf16[1024,1280]{0,1:T(8,128)(2,1)}) %all-gather.3.cloned.1.call-update) | async-done | bytes 2621456 | tf_op jit(solution)/shard_map/all_gather | solution.py:77
  41.4 16.3 %fusion = (f32[1024,2,5]{0,2,1:T(8,128)S(1)}, f32[2,896,1024,5]{2,1,3,0:T(8,128)}) fusion(pred[1024,896]{0,1:T(8,128)(4,1)S(1)} %bitcast_compare_fusion, bf16[896,2,128,1]{0,2,3,1:T(8,128)(2,1)S(1)} %bitcast.144, bf16[1024,2,5,128]{0,3,2,1:T(8,128)(2,1)} %bitcast.138), kind=kOutput, calls=%fused_computation.2 | convolution fusion | flops 2376325120 | bytes 40738816 | tf_op jit(solution)/shard_map/tgrd,kgd->tgrk/dot_general | solution.py:18
  57.7 0.4 broadcast_in_dim.146
  58.2 1.8 copy-done.1
  60.0 15.7 %fusion.4 = f32[1024,2,5]{0,2,1:T(8,128)S(1)} fusion(f32[2,896,1024,5]{2,1,3,0:T(8,128)} %get-tuple-element.20, f32[1024,896]{0,1:T(8,128)S(1)} %bitcast.133, f32[1024,2,5]{0,2,1:T(8,128)S(1)} %get-tuple-element.14, pred[1024,896]{0,1:T(8,128)(4,1)S(1)} %bitcast_compare_fusion), kind=kLoop, calls=%fused_computation.6 | loop fusion | flops 45864960 | bytes 41369600 | tf_op jit(solution)/shard_map/reduce_sum | solution.py:26
  75.7 0.6 copy.164
  76.3 4.0 all-to-all-start.2
  80.4 0.8 copy.146
  81.2 0.2 copy.155
  81.4 0.6 copy.144
  82.1 3.8 all-to-all-done.2
  85.8 3.3 all-to-all-start
  89.2 17.4 %bitcast_add_fusion = f32[1024,2,5,128]{3,0,2,1:T(8,128)S(1)} fusion(f32[1024,2,5]{0,2,1:T(8,128)S(1)} %get-tuple-element.13, bf16[896,2,128,1]{0,2,3,1:T(8,128)(2,1)S(1)} %bitcast.150, f32[2,896,1024,5]{2,1,3,0:T(8,128)} %get-tuple-element.20, f32[1024,896]{0,1:T(8,128)} %bitcast.134, f32[1024,2,5]{0,2,1:T(8,128)S(1)} %get-tuple-element.14, ...), kind=kOutput, calls=%fused_computation.21 | convolution fusion | flops 2395996160 | bytes 47071232 | tf_op jit(solution)/shard_map/tgrk,kgd->tgrd/dot_general | solution.py:27
  106.7 2.7 copy.158
  109.4 5.0 all-to-all-start.1
  114.5 0.1 convolution_convert_fusion.2
  114.6 0.1 fusion.47
  114.8 0.3 broadcast_compare_fusion
  115.1 15.4 %all-gather.5.cloned.1.call-done = bf16[2048,512]{0,1:T(8,128)(2,1)} async-done(((bf16[128,512]{0,1:T(8,128)(2,1)}), bf16[2048,512]{0,1:T(8,128)(2,1)}) %all-gather.5.cloned.1.call-update) | async-done | bytes 2097168 | tf_op jit(solution)/shard_map/all_gather | solution.py:127
  130.5 2.7 fusion.68
  133.2 5.8 %fusion.9 = (f32[128,2,5]{0,2,1:T(8,128)S(1)}, f32[2,2048,128,5]{2,1,3,0:T(8,128)}) fusion(pred[128,2048]{0,1:T(8,128)(4,1)S(1)} %get-tuple-element.17, bf16[2048,2,128,1]{0,2,3,1:T(8,128)(2,1)S(1)} %bitcast.141, bf16[128,2,5,128]{0,3,2,1:T(8,128)(2,1)S(1)} %bitcast.140), kind=kOutput, calls=%fused_computation.14 | convolution fusion | flops 678951680 | bytes 12129280 | tf_op jit(solution)/shard_map/tgrd,kgd->tgrk/dot_general | solution.py:18
  139.2 6.4 %fusion.13 = f32[128,2,5]{0,2,1:T(8,128)S(1)} fusion(f32[2,2048,128,5]{2,1,3,0:T(8,128)} %get-tuple-element.22, f32[128,2048]{0,1:T(8,128)S(1)} %get-tuple-element.18, f32[128,2,5]{0,2,1:T(8,128)S(1)} %copy.161, pred[128,2048]{0,1:T(8,128)(4,1)S(1)} %get-tuple-element.17), kind=kLoop, calls=%fused_computation.18 | loop fusion | flops 13105920 | bytes 11806720 | tf_op jit(solution)/shard_map/reduce_sum | solution.py:26
  145.7 29.6 %all-to-all-done.1 = f32[8,128,2,5,128]{4,1,3,2,0:T(8,128)} async-done(((f32[8,128,2,5,128]{4,1,3,2,0:T(8,128)}), f32[8,128,2,5,128]{4,1,3,2,0:T(8,128)}, u32[]{:S(2)}, u32[]{:S(2)}) %all-to-all-start.1) | async-done | bytes 5242912 | tf_op jit(solution)/shard_map/all_to_all | solution.py:114
  175.3 4.3 multiply_reduce_fusion
  179.6 2.2 copy.160
  181.8 7.9 %fusion.42 = bf16[128,2,5,128]{0,3,2,1:T(8,128)(2,1)S(1)} fusion(bf16[2048,2,128,1]{0,2,3,1:T(8,128)(2,1)} %bitcast.147, f32[2,2048,128,5]{2,1,3,0:T(8,128)} %get-tuple-element.22, f32[128,2048]{0,1:T(8,128)} %copy-done.4, f32[128,2,5]{0,2,1:T(8,128)S(1)} %copy.161, pred[128,2048]{0,1:T(8,128)(4,1)S(1)} %get-tuple-element.17, ...), kind=kOutput, calls=%fused_computation.49 | convolution fusion | flops 684851200 | bytes 13843456 | tf_op jit(solution)/shard_map/tgrk,kgd->tgrd/dot_general | solution.py:27
  189.7 1.0 fusion.25
  190.7 0.2 fusion.29
  191.0 3.2 convolution_convert_fusion.1
  194.3 126.3 %all_to_all.25 = bf16[128,16,2560]{2,1,0:T(8,128)(2,1)S(1)} all-to-all(bf16[128,16,2560]{2,1,0:T(8,128)(2,1)S(1)} %bitcast.130), channel_id=1, replica_groups=mesh['req'=8,'exp'=16] {'req','exp'}, dimensions={0} | all-to-all | bytes 20971520 | tf_op jit(solution)/shard_map/all_to_all | solution.py:175
  320.5 3.8 copy-done.2
  324.4 10.2 %fusion.21 = f32[2048,768]{1,0:T(8,128)} fusion(bf16[2048,2560]{1,0:T(8,128)(2,1)S(1)} %bitcast.136, bf16[1,2560,768]{2,1,0:T(8,128)(2,1)S(1)} %copy-done.8), kind=kOutput, calls=%fused_computation.27 | convolution fusion | flops 8053063680 | bytes 20709376 | tf_op jit(solution)/shard_map/dot_general | solution.py:178
  334.5 28.9 %convolution_convert_fusion = bf16[2048,2560]{1,0:T(8,128)(2,1)} fusion(f32[2048,768]{1,0:T(8,128)} %fusion.21, bf16[2048,2560]{1,0:T(8,128)(2,1)} %bitcast.137, bf16[1,768,2560]{2,1,0:T(8,128)(2,1)} %param.23, bf16[1,2560,768]{2,1,0:T(8,128)(2,1)} %param.22), kind=kOutput, calls=%fused_computation.10 | convolution fusion | flops 16120807424 | bytes 35127296 | tf_op jit(solution)/shard_map/dot_general | solution.py:182
  363.5 6.7 %all-to-all-start.4 = ((bf16[128,16,2560]{2,1,0:T(8,128)(2,1)}), bf16[128,16,2560]{2,1,0:T(8,128)(2,1)}, u32[]{:S(2)}, u32[]{:S(2)}) async-start(bf16[128,16,2560]{2,1,0:T(8,128)(2,1)} %bitcast.135), calls=%async_computation.4 | async-start | bytes 20971520 | tf_op jit(solution)/shard_map/all_to_all | solution.py:181
  370.1 0.4 fusion.49
  370.7 0.1 select_convert_fusion
  370.8 0.1 fusion.45
  371.0 141.3 %all-to-all-done.4 = bf16[128,16,2560]{2,1,0:T(8,128)(2,1)} async-done(((bf16[128,16,2560]{2,1,0:T(8,128)(2,1)}), bf16[128,16,2560]{2,1,0:T(8,128)(2,1)}, u32[]{:S(2)}, u32[]{:S(2)}) %all-to-all-start.4) | async-done | bytes 10485792 | tf_op jit(solution)/shard_map/all_to_all | solution.py:181
  512.3 5.5 %fusion.70 = f32[128,2560]{1,0:T(8,128)S(1)} fusion(bf16[128,2048]{0,1:T(8,128)(2,1)S(1)} %bitcast.143, bf16[2048,2560]{1,0:T(8,128)(2,1)} %bitcast.34), kind=kOutput, calls=%fused_computation.101 | convolution fusion | flops 1342177280 | bytes 12320768 | tf_op jit(solution)/shard_map/dot_general | solution.py:198
  518.0 6.4 %fusion.24 = bf16[128,2560]{1,0:T(8,128)(2,1)} fusion(f32[128,2560]{1,0:T(8,128)S(1)} %fusion.70, bf16[128,2048]{0,1:T(8,128)(2,1)S(1)} %bitcast.142, bf16[2048,2560]{1,0:T(8,128)(2,1)} %bitcast.34, bf16[128,2560]{1,0:T(8,128)(2,1)S(1)} %fusion.25), kind=kOutput, calls=%fused_computation.32 | convolution fusion | flops 1343488000 | bytes 13631488 | tf_op jit(solution)/shard_map/dot_general | solution.py:198
  (57 shorter events, 0.9 us)
Async XLA Ops:
  7.4 362.8 %copy-start = (bf16[2560,64]{0,1:T(8,128)(2,1)S(1)}, bf16[2560,64]{0,1:T(8,128)(2,1)}, u32[]{:S(2)}) copy-start(bf16[2560,64]{0,1:T(8,128)(2,1)} %param.19) | copy-start | bytes 983044
  7.4 34.0 %all-gather.3.cloned.1.call-start = ((), (), s32[]{:S(2)}) async-start(), calls=%async_computation.5 | async-start | bytes 2949120 | tf_op jit(solution)/shard_map/all_gather | solution.py:77
  58.2 1.8 copy-start.1
  60.0 20.4 %copy-start.6 = (bf16[128,512]{1,0:T(8,128)(2,1)S(1)}, bf16[128,512]{1,0:T(8,128)(2,1)}, u32[]{:S(2)}) copy-start(bf16[128,512]{1,0:T(8,128)(2,1)} %param.14) | copy-start | bytes 393220
  76.3 9.5 %all-to-all-start.2 = ((f32[8,128,2,5]{1,2,3,0:T(2,128)}), f32[8,128,2,5]{1,2,3,0:T(2,128)S(1)}, u32[]{:S(2)}, u32[]{:S(2)}) async-start(f32[8,128,2,5]{1,2,3,0:T(2,128)} %copy.164), calls=%async_computation.2 | async-start | bytes 81920 | tf_op jit(solution)/shard_map/all_to_all | solution.py:107
  80.3 50.2 %all-gather.5.cloned.1.call-start = ((), (), s32[]{:S(2)}) async-start(), calls=%async_computation.6 | async-start | bytes 2228224 | tf_op jit(solution)/shard_map/all_gather | solution.py:127
  85.8 23.6 %all-to-all-start = ((f32[8,128,2,5]{1,2,3,0:T(2,128)}), f32[8,128,2,5]{1,2,3,0:T(2,128)S(1)}, u32[]{:S(2)}, u32[]{:S(2)}) async-start(f32[8,128,2,5]{1,2,3,0:T(2,128)} %copy.144), calls=%async_computation | async-start | bytes 81920 | tf_op jit(solution)/shard_map/all_to_all | solution.py:100
  106.6 7.7 %copy-start.9 = (s32[1,4]{1,0:T(1,128)S(1)}, s32[1,4]{1,0:T(1,128)}, u32[]{:S(2)}) copy-start(s32[1,4]{1,0:T(1,128)} %param.15) | copy-start | bytes 52
  106.6 7.8 %copy-start.7 = (s32[128,6]{0,1:T(8,128)S(1)}, s32[128,6]{0,1:T(8,128)}, u32[]{:S(2)}) copy-start(s32[128,6]{0,1:T(8,128)} %param.20) | copy-start | bytes 9220
  109.4 23.9 %copy-start.3 = (bf16[128,1280]{0,1:T(8,128)(2,1)S(1)}, bf16[128,1280]{0,1:T(8,128)(2,1)}, u32[]{:S(2)}) copy-start(bf16[128,1280]{0,1:T(8,128)(2,1)} %copy.140) | copy-start | bytes 983044
  109.4 65.9 %all-to-all-start.1 = ((f32[8,128,2,5,128]{4,1,3,2,0:T(8,128)}), f32[8,128,2,5,128]{4,1,3,2,0:T(8,128)}, u32[]{:S(2)}, u32[]{:S(2)}) async-start(f32[8,128,2,5,128]{4,1,3,2,0:T(8,128)} %copy.158), calls=%async_computation.1 | async-start | bytes 10485760 | tf_op jit(solution)/shard_map/all_to_all | solution.py:114
  115.1 24.1 %copy-start.4 = (f32[128,2048]{0,1:T(8,128)}, f32[128,2048]{0,1:T(8,128)S(1)}, u32[]{:S(2)}) copy-start(f32[128,2048]{0,1:T(8,128)S(1)} %get-tuple-element.18) | copy-start | bytes 3145732
  175.3 14.4 %slice-start = ((s8[6553600]{0:T(1024)(128)(4,1)}), s8[2359296]{0:T(1024)(128)(4,1)S(1)}, s32[]{:S(2)}) async-start(s8[6553600]{0:T(1024)(128)(4,1)} %bitcast.131), calls=%async_computation.7 | async-start | bytes 4718592
  181.8 7.9 %slice-start.1 = ((s8[6553600]{0:T(1024)(128)(4,1)}), s8[4194304]{0:T(1024)(128)(4,1)S(1)}, s32[]{:S(2)}) async-start(s8[6553600]{0:T(1024)(128)(4,1)} %bitcast.131), calls=%async_computation.8 | async-start | bytes 8388608
  181.8 7.9 %copy-start.5 = (bf16[128,2560]{1,0:T(8,128)(2,1)S(1)}, bf16[128,2560]{1,0:T(8,128)(2,1)}, u32[]{:S(2)}) copy-start(bf16[128,2560]{1,0:T(8,128)(2,1)} %param.12) | copy-start | bytes 1966084
  194.3 130.1 %copy-start.8 = (bf16[1,2560,768]{2,1,0:T(8,128)(2,1)S(1)}, bf16[1,2560,768]{2,1,0:T(8,128)(2,1)}, u32[]{:S(2)}) copy-start(bf16[1,2560,768]{2,1,0:T(8,128)(2,1)} %param.21) | copy-start | bytes 11796484
  320.5 3.8 copy-start.2
  363.5 148.8 %all-to-all-start.4 = ((bf16[128,16,2560]{2,1,0:T(8,128)(2,1)}), bf16[128,16,2560]{2,1,0:T(8,128)(2,1)}, u32[]{:S(2)}, u32[]{:S(2)}) async-start(bf16[128,16,2560]{2,1,0:T(8,128)(2,1)} %bitcast.135), calls=%async_computation.4 | async-start | bytes 20971520 | tf_op jit(solution)/shard_map/all_to_all | solution.py:181
Sparse Core Ops, SparseCore 0:
  9.9 31.4 all-gather.2
Sparse Core Ops, SparseCore 1:
  82.9 47.5 all-gather.4
where the time goes:
time: 533 us; the launch traced here: 532 us
  waiting for transfers between devices  206 us (39%)
  blocking collectives  138 us (26%)
  matrix products  104 us (20%)
  other arithmetic  29.7 us (6%)
  local copies, waits for them, and re-layouts  19.7 us (4%)
  starting transfers between devices  19 us (4%)
  between operations  15.2 us (3%)
    all_to_all x1, waiting for transfers between devices, on_device(): lax.all_to_all(jnp.dot(inner, w_down[0], preferred_element_type=jnp.float...  141 us
    all_to_all x1, blocking collectives, on_device(): lax.all_to_all(outgoing, ('req', 'exp'), split_axis=0, concat_axis=0, til...  126 us
    all_to_all x1, waiting for transfers between devices, on_device(): lax.all_to_all(summed_output.reshape(request_count, token_index, KEY_VALU...  29.6 us
    dot_general x1, matrix products, on_device(): jnp.dot(inner, w_down[0], preferred_element_type=jnp.float32)  28.9 us
    dot_general x2, matrix products, fold_scores(): jnp.einsum('tgrk,kgd->tgrd', expo.astype(jnp.bfloat16), value_rows, prefe...  25.3 us
    dot_general x2, matrix products, fold_scores(): jnp.einsum('tgrd,kgd->tgrk', query_matrix, key_rows, preferred_element_ty...  22.1 us
    reduce_sum x2, other arithmetic, fold_scores(): grand_total = decay * grand_total + jnp.sum(expo, axis=-1)  22.1 us
    all_gather x1, waiting for transfers between devices, on_device(): lax.all_gather(queries, 'req', axis=0, tiled=True)  16.3 us
  transfers between devices with their start and end apart: 6, of which 5 were waited for; matrix products, arithmetic and copies ran while one was open for 8% of the time, Pallas kernels for 0%

commit v1 on v0

--- a/solution.py
+++ b/solution.py
@@ -12,6 +12,11 @@
 PAGE_TOKENS = 128
 NEGATIVE_MASK = -1e30
 EPS = 1e-06
+
+
+def gather_by_exchange(array, axis, dim):
+    copies = jnp.concatenate([array] * lax.axis_size(axis), axis=dim)
+    return lax.all_to_all(copies, axis, dim, dim, tiled=True)
 
 
 def fold_scores(carry, query_matrix, key_rows, value_rows, weights):
@@ -75,7 +80,7 @@
     query_counts = jnp.dot(pick.astype(jnp.float32), counts, precision=lax.Precision.HIGHEST)
     query_total_set, every_count = (
         lax.all_gather(queries, "req", axis=0, tiled=True),
-        lax.all_gather(query_counts.astype(jnp.bfloat16), "req", axis=0, tiled=True),
+        gather_by_exchange(query_counts.astype(jnp.bfloat16), "req", 0),
     )
     query_total_count = query_total_set.shape[0]
     local = lax.dynamic_slice_in_dim(

time: 533 us -> 533 us (level)
  blocking collectives: 138 us -> 126 us
  waiting for transfers between devices: 206 us -> 213 us
    all_gather x1 -> x0, blocking collectives: 12.1 us -> none  [on_device(): lax.all_gather(query_counts.astype(jnp.bfloat16), 'req', axis=0, tiled=True)]
  transfers between devices with their start and end apart: 6 -> 7, of which waited for: 5 -> 6; matrix products, arithmetic and copies ran while one was open for 8% -> 8% of each run, Pallas kernels for 0% -> 0%
where the time goes in v1:
time: 533 us; the launch traced here: 532 us
  waiting for transfers between devices  213 us (40%)
  blocking collectives  126 us (24%)
  matrix products  104 us (20%)
  other arithmetic  29.7 us (6%)
  starting transfers between devices  23.4 us (4%)
  local copies, waits for them, and re-layouts  20.4 us (4%)
  between operations  15.3 us (3%)
    all_to_all x1, waiting for transfers between devices, on_device(): lax.all_to_all(jnp.dot(inner, w_down[0], preferred_element_type=jnp.float...  141 us
    all_to_all x1, blocking collectives, on_device(): lax.all_to_all(outgoing, ('req', 'exp'), split_axis=0, concat_axis=0, til...  126 us
    all_to_all x1, waiting for transfers between devices, on_device(): lax.all_to_all(summed_output.reshape(request_count, token_index, KEY_VALU...  29.6 us
    dot_general x1, matrix products, on_device(): jnp.dot(inner, w_down[0], preferred_element_type=jnp.float32)  28.9 us
    dot_general x2, matrix products, fold_scores(): jnp.einsum('tgrk,kgd->tgrd', expo.astype(jnp.bfloat16), value_rows, prefe...  25.3 us
    dot_general x2, matrix products, fold_scores(): jnp.einsum('tgrd,kgd->tgrk', query_matrix, key_rows, preferred_element_ty...  22.1 us
    reduce_sum x2, other arithmetic, fold_scores(): grand_total = decay * grand_total + jnp.sum(expo, axis=-1)  22.1 us
    all_gather x1, waiting for transfers between devices, on_device(): lax.all_gather(queries, 'req', axis=0, tiled=True)  18.6 us
  transfers between devices with their start and end apart: 7, of which 6 were waited for; matrix products, arithmetic and copies ran while one was open for 8% of the time, Pallas kernels for 0%

profile of v1, /device:TPU:34, one launch (start us, length us, event | category | flops | bytes accessed | tf_op | source)
XLA Modules:
  0.0 531.8 jit_solution(5143239296382281209)
XLA Ops:
  7.4 1.9 copy.176
  9.3 0.8 reduce-window.4
  10.2 0.8 convert_reduce_fusion
  11.0 0.2 constant_dynamic-update-slice_fusion.7
  11.3 0.7 copy_bitcast_fusion.1
  12.0 4.5 all-to-all-start
  16.5 1.2 fusion.69
  17.7 0.2 copy.175
  17.9 4.5 all-to-all-done
  22.5 0.2 bitcast_compare_fusion
  22.7 18.6 %all-gather.3.cloned.1.call-done = bf16[1024,1280]{0,1:T(8,128)(2,1)} async-done(((bf16[128,1280]{0,1:T(8,128)(2,1)}), bf16[1024,1280]{0,1:T(8,128)(2,1)}) %all-gather.3.cloned.1.call-update) | async-done | bytes 2621456 | tf_op jit(solution)/shard_map/all_gather | solution.py:82
  41.4 16.3 %fusion = (f32[1024,2,5]{0,2,1:T(8,128)S(1)}, f32[2,896,1024,5]{2,1,3,0:T(8,128)}) fusion(pred[1024,896]{0,1:T(8,128)(4,1)S(1)} %bitcast_compare_fusion, bf16[896,2,128,1]{0,2,3,1:T(8,128)(2,1)S(1)} %bitcast.154, bf16[1024,2,5,128]{0,3,2,1:T(8,128)(2,1)} %bitcast.148), kind=kOutput, calls=%fused_computation.2 | convolution fusion | flops 2376325120 | bytes 40738816 | tf_op jit(solution)/shard_map/tgrd,kgd->tgrk/dot_general | solution.py:23
  57.7 0.4 broadcast_in_dim.146
  58.2 1.8 copy-done.1
  60.0 15.7 %fusion.4 = f32[1024,2,5]{0,2,1:T(8,128)S(1)} fusion(f32[2,896,1024,5]{2,1,3,0:T(8,128)} %get-tuple-element.22, f32[1024,896]{0,1:T(8,128)S(1)} %bitcast.143, f32[1024,2,5]{0,2,1:T(8,128)S(1)} %get-tuple-element.14, pred[1024,896]{0,1:T(8,128)(4,1)S(1)} %bitcast_compare_fusion), kind=kLoop, calls=%fused_computation.6 | loop fusion | flops 45864960 | bytes 41369600 | tf_op jit(solution)/shard_map/reduce_sum | solution.py:31
  75.7 0.6 copy.200
  76.3 4.0 all-to-all-start.3
  80.4 0.8 copy.182
  81.2 0.2 copy.191
  81.4 0.6 copy.180
  82.1 3.8 all-to-all-done.3
  85.8 3.3 all-to-all-start.1
  89.2 17.4 %bitcast_add_fusion = f32[1024,2,5,128]{3,0,2,1:T(8,128)S(1)} fusion(f32[1024,2,5]{0,2,1:T(8,128)S(1)} %get-tuple-element.13, bf16[896,2,128,1]{0,2,3,1:T(8,128)(2,1)S(1)} %bitcast.160, f32[2,896,1024,5]{2,1,3,0:T(8,128)} %get-tuple-element.22, f32[1024,896]{0,1:T(8,128)} %bitcast.144, f32[1024,2,5]{0,2,1:T(8,128)S(1)} %get-tuple-element.14, ...), kind=kOutput, calls=%fused_computation.21 | convolution fusion | flops 2395996160 | bytes 47071232 | tf_op jit(solution)/shard_map/tgrk,kgd->tgrd/dot_general | solution.py:32
  106.7 2.7 copy.194
  109.4 5.0 all-to-all-start.2
  114.5 0.1 convolution_convert_fusion.2
  114.8 0.3 broadcast_compare_fusion
  115.1 15.4 %all-gather.5.cloned.1.call-done = bf16[2048,512]{0,1:T(8,128)(2,1)} async-done(((bf16[128,512]{0,1:T(8,128)(2,1)}), bf16[2048,512]{0,1:T(8,128)(2,1)}) %all-gather.5.cloned.1.call-update) | async-done | bytes 2097168 | tf_op jit(solution)/shard_map/all_gather | solution.py:132
  130.5 2.7 fusion.68
  133.2 5.8 %fusion.9 = (f32[128,2,5]{0,2,1:T(8,128)S(1)}, f32[2,2048,128,5]{2,1,3,0:T(8,128)}) fusion(pred[128,2048]{0,1:T(8,128)(4,1)S(1)} %get-tuple-element.17, bf16[2048,2,128,1]{0,2,3,1:T(8,128)(2,1)S(1)} %bitcast.151, bf16[128,2,5,128]{0,3,2,1:T(8,128)(2,1)S(1)} %bitcast.150), kind=kOutput, calls=%fused_computation.14 | convolution fusion | flops 678951680 | bytes 12129280 | tf_op jit(solution)/shard_map/tgrd,kgd->tgrk/dot_general | solution.py:23
  139.2 6.4 %fusion.13 = f32[128,2,5]{0,2,1:T(8,128)S(1)} fusion(f32[2,2048,128,5]{2,1,3,0:T(8,128)} %get-tuple-element.24, f32[128,2048]{0,1:T(8,128)S(1)} %get-tuple-element.18, f32[128,2,5]{0,2,1:T(8,128)S(1)} %copy.197, pred[128,2048]{0,1:T(8,128)(4,1)S(1)} %get-tuple-element.17), kind=kLoop, calls=%fused_computation.18 | loop fusion | flops 13105920 | bytes 11806720 | tf_op jit(solution)/shard_map/reduce_sum | solution.py:31
  145.7 29.6 %all-to-all-done.2 = f32[8,128,2,5,128]{4,1,3,2,0:T(8,128)} async-done(((f32[8,128,2,5,128]{4,1,3,2,0:T(8,128)}), f32[8,128,2,5,128]{4,1,3,2,0:T(8,128)}, u32[]{:S(2)}, u32[]{:S(2)}) %all-to-all-start.2) | async-done | bytes 5242912 | tf_op jit(solution)/shard_map/all_to_all | solution.py:119
  175.3 4.3 multiply_reduce_fusion
  179.6 2.2 copy.196
  181.8 7.9 %fusion.42 = bf16[128,2,5,128]{0,3,2,1:T(8,128)(2,1)S(1)} fusion(bf16[2048,2,128,1]{0,2,3,1:T(8,128)(2,1)} %bitcast.157, f32[2,2048,128,5]{2,1,3,0:T(8,128)} %get-tuple-element.24, f32[128,2048]{0,1:T(8,128)} %copy-done.4, f32[128,2,5]{0,2,1:T(8,128)S(1)} %copy.197, pred[128,2048]{0,1:T(8,128)(4,1)S(1)} %get-tuple-element.17, ...), kind=kOutput, calls=%fused_computation.49 | convolution fusion | flops 684851200 | bytes 13843456 | tf_op jit(solution)/shard_map/tgrk,kgd->tgrd/dot_general | solution.py:32
  189.7 1.0 fusion.25
  190.7 0.2 fusion.29
  191.0 3.2 convolution_convert_fusion.1
  194.3 126.3 %all_to_all.37 = bf16[128,16,2560]{2,1,0:T(8,128)(2,1)S(1)} all-to-all(bf16[128,16,2560]{2,1,0:T(8,128)(2,1)S(1)} %bitcast.140), channel_id=1, replica_groups=mesh['req'=8,'exp'=16] {'req','exp'}, dimensions={0} | all-to-all | bytes 20971520 | tf_op jit(solution)/shard_map/all_to_all | solution.py:180
  320.5 3.8 copy-done.2
  324.4 10.2 %fusion.21 = f32[2048,768]{1,0:T(8,128)} fusion(bf16[2048,2560]{1,0:T(8,128)(2,1)S(1)} %bitcast.146, bf16[1,2560,768]{2,1,0:T(8,128)(2,1)S(1)} %copy-done.8), kind=kOutput, calls=%fused_computation.27 | convolution fusion | flops 8053063680 | bytes 20709376 | tf_op jit(solution)/shard_map/dot_general | solution.py:183
  334.5 28.9 %convolution_convert_fusion = bf16[2048,2560]{1,0:T(8,128)(2,1)} fusion(f32[2048,768]{1,0:T(8,128)} %fusion.21, bf16[2048,2560]{1,0:T(8,128)(2,1)} %bitcast.147, bf16[1,768,2560]{2,1,0:T(8,128)(2,1)} %param.23, bf16[1,2560,768]{2,1,0:T(8,128)(2,1)} %param.22), kind=kOutput, calls=%fused_computation.10 | convolution fusion | flops 16120807424 | bytes 35127296 | tf_op jit(solution)/shard_map/dot_general | solution.py:187
  363.5 6.7 %all-to-all-start.5 = ((bf16[128,16,2560]{2,1,0:T(8,128)(2,1)}), bf16[128,16,2560]{2,1,0:T(8,128)(2,1)}, u32[]{:S(2)}, u32[]{:S(2)}) async-start(bf16[128,16,2560]{2,1,0:T(8,128)(2,1)} %bitcast.145), calls=%async_computation.5 | async-start | bytes 20971520 | tf_op jit(solution)/shard_map/all_to_all | solution.py:186
  370.1 0.4 fusion.49
  370.8 0.1 fusion.45
  371.0 141.3 %all-to-all-done.5 = bf16[128,16,2560]{2,1,0:T(8,128)(2,1)} async-done(((bf16[128,16,2560]{2,1,0:T(8,128)(2,1)}), bf16[128,16,2560]{2,1,0:T(8,128)(2,1)}, u32[]{:S(2)}, u32[]{:S(2)}) %all-to-all-start.5) | async-done | bytes 10485792 | tf_op jit(solution)/shard_map/all_to_all | solution.py:186
  512.3 5.5 %fusion.70 = f32[128,2560]{1,0:T(8,128)S(1)} fusion(bf16[128,2048]{0,1:T(8,128)(2,1)S(1)} %bitcast.153, bf16[2048,2560]{1,0:T(8,128)(2,1)} %bitcast.34), kind=kOutput, calls=%fused_computation.111 | convolution fusion | flops 1342177280 | bytes 12320768 | tf_op jit(solution)/shard_map/dot_general | solution.py:203
  518.0 6.4 %fusion.24 = bf16[128,2560]{1,0:T(8,128)(2,1)} fusion(f32[128,2560]{1,0:T(8,128)S(1)} %fusion.70, bf16[128,2048]{0,1:T(8,128)(2,1)S(1)} %bitcast.152, bf16[2048,2560]{1,0:T(8,128)(2,1)} %bitcast.34, bf16[128,2560]{1,0:T(8,128)(2,1)S(1)} %fusion.25), kind=kOutput, calls=%fused_computation.32 | convolution fusion | flops 1343488000 | bytes 13631488 | tf_op jit(solution)/shard_map/dot_general | solution.py:203
  (67 shorter events, 1.2 us)
Async XLA Ops:
  7.4 362.8 %copy-start = (bf16[2560,64]{0,1:T(8,128)(2,1)S(1)}, bf16[2560,64]{0,1:T(8,128)(2,1)}, u32[]{:S(2)}) copy-start(bf16[2560,64]{0,1:T(8,128)(2,1)} %param.19) | copy-start | bytes 983044
  7.4 34.0 %all-gather.3.cloned.1.call-start = ((), (), s32[]{:S(2)}) async-start(), calls=%async_computation.6 | async-start | bytes 2949120 | tf_op jit(solution)/shard_map/all_gather | solution.py:82
  12.0 10.4 %all-to-all-start = ((bf16[8,128,56]{1,2,0:T(8,128)(2,1)}), bf16[8,128,56]{1,2,0:T(8,128)(2,1)S(1)}, u32[]{:S(2)}, u32[]{:S(2)}) async-start(bf16[8,128,56]{1,2,0:T(8,128)(2,1)} %copy_bitcast_fusion.1), calls=%async_computation | async-start | bytes 229376 | tf_op jit(solution)/shard_map/all_to_all | solution.py:19
  58.2 1.8 copy-start.1
  60.0 20.4 %copy-start.6 = (bf16[128,512]{1,0:T(8,128)(2,1)S(1)}, bf16[128,512]{1,0:T(8,128)(2,1)}, u32[]{:S(2)}) copy-start(bf16[128,512]{1,0:T(8,128)(2,1)} %param.14) | copy-start | bytes 393220
  76.3 9.5 %all-to-all-start.3 = ((f32[8,128,2,5]{1,2,3,0:T(2,128)}), f32[8,128,2,5]{1,2,3,0:T(2,128)S(1)}, u32[]{:S(2)}, u32[]{:S(2)}) async-start(f32[8,128,2,5]{1,2,3,0:T(2,128)} %copy.200), calls=%async_computation.3 | async-start | bytes 81920 | tf_op jit(solution)/shard_map/all_to_all | solution.py:112
  80.3 50.2 %all-gather.5.cloned.1.call-start = ((), (), s32[]{:S(2)}) async-start(), calls=%async_computation.7 | async-start | bytes 2228224 | tf_op jit(solution)/shard_map/all_gather | solution.py:132
  85.8 23.6 %all-to-all-start.1 = ((f32[8,128,2,5]{1,2,3,0:T(2,128)}), f32[8,128,2,5]{1,2,3,0:T(2,128)S(1)}, u32[]{:S(2)}, u32[]{:S(2)}) async-start(f32[8,128,2,5]{1,2,3,0:T(2,128)} %copy.180), calls=%async_computation.1 | async-start | bytes 81920 | tf_op jit(solution)/shard_map/all_to_all | solution.py:105
  106.6 7.7 %copy-start.9 = (s32[1,4]{1,0:T(1,128)S(1)}, s32[1,4]{1,0:T(1,128)}, u32[]{:S(2)}) copy-start(s32[1,4]{1,0:T(1,128)} %param.15) | copy-start | bytes 52
  106.6 7.8 %copy-start.7 = (s32[128,6]{0,1:T(8,128)S(1)}, s32[128,6]{0,1:T(8,128)}, u32[]{:S(2)}) copy-start(s32[128,6]{0,1:T(8,128)} %param.20) | copy-start | bytes 9220
  109.4 23.9 %copy-start.3 = (bf16[128,1280]{0,1:T(8,128)(2,1)S(1)}, bf16[128,1280]{0,1:T(8,128)(2,1)}, u32[]{:S(2)}) copy-start(bf16[128,1280]{0,1:T(8,128)(2,1)} %copy.176) | copy-start | bytes 983044
  109.4 65.9 %all-to-all-start.2 = ((f32[8,128,2,5,128]{4,1,3,2,0:T(8,128)}), f32[8,128,2,5,128]{4,1,3,2,0:T(8,128)}, u32[]{:S(2)}, u32[]{:S(2)}) async-start(f32[8,128,2,5,128]{4,1,3,2,0:T(8,128)} %copy.194), calls=%async_computation.2 | async-start | bytes 10485760 | tf_op jit(solution)/shard_map/all_to_all | solution.py:119
  115.1 24.1 %copy-start.4 = (f32[128,2048]{0,1:T(8,128)}, f32[128,2048]{0,1:T(8,128)S(1)}, u32[]{:S(2)}) copy-start(f32[128,2048]{0,1:T(8,128)S(1)} %get-tuple-element.18) | copy-start | bytes 3145732
  175.3 14.4 %slice-start = ((s8[6553600]{0:T(1024)(128)(4,1)}), s8[2359296]{0:T(1024)(128)(4,1)S(1)}, s32[]{:S(2)}) async-start(s8[6553600]{0:T(1024)(128)(4,1)} %bitcast.141), calls=%async_computation.8 | async-start | bytes 4718592
  181.8 7.9 %slice-start.1 = ((s8[6553600]{0:T(1024)(128)(4,1)}), s8[4194304]{0:T(1024)(128)(4,1)S(1)}, s32[]{:S(2)}) async-start(s8[6553600]{0:T(1024)(128)(4,1)} %bitcast.141), calls=%async_computation.9 | async-start | bytes 8388608
  181.8 7.9 %copy-start.5 = (bf16[128,2560]{1,0:T(8,128)(2,1)S(1)}, bf16[128,2560]{1,0:T(8,128)(2,1)}, u32[]{:S(2)}) copy-start(bf16[128,2560]{1,0:T(8,128)(2,1)} %param.12) | copy-start | bytes 1966084
  194.3 130.1 %copy-start.8 = (bf16[1,2560,768]{2,1,0:T(8,128)(2,1)S(1)}, bf16[1,2560,768]{2,1,0:T(8,128)(2,1)}, u32[]{:S(2)}) copy-start(bf16[1,2560,768]{2,1,0:T(8,128)(2,1)} %param.21) | copy-start | bytes 11796484
  320.5 3.8 copy-start.2
  363.5 148.8 %all-to-all-start.5 = ((bf16[128,16,2560]{2,1,0:T(8,128)(2,1)}), bf16[128,16,2560]{2,1,0:T(8,128)(2,1)}, u32[]{:S(2)}, u32[]{:S(2)}) async-start(bf16[128,16,2560]{2,1,0:T(8,128)(2,1)} %bitcast.145), calls=%async_computation.5 | async-start | bytes 20971520 | tf_op jit(solution)/shard_map/all_to_all | solution.py:186
Sparse Core Ops, SparseCore 0:
  9.9 31.4 all-gather.2
Sparse Core Ops, SparseCore 1:
  82.9 47.5 all-gather.4
